TPU v7x, 128 devices: a whole 4x4x4 slice. The times are simulated.
128 devices in a mesh: ma: 16 (over x, z), band: 8 (over y, core).
Axes of the slice: x: 4, y: 4, z: 4, core: 2. Of those that a mesh axis runs over, the one named last changes fastest.
Arguments:
- harmonics: bfloat16 [128, 8192, 256], P(('ma', 'band')), may hold values from -6 to 6
- legendre: bfloat16 [128, 2, 8192, 512], P(('ma', 'band')), may hold values from -0.0029296875 to 0.0029296875
- m_values: int32 [128], replicated, may hold values from 1 to 8191
- cycle_cell: int32 [16384], P(('ma', 'band')), may hold values from 0 to 63, as said below
- phi_cell: int32 [16384], P(('ma', 'band')), may hold values from 3 to 123
- offsets: float32 [2, 16384], P(None, ('ma', 'band')), may hold values from 0 to 1
Outputs:
- lensed: float32 [16384, 128], P(('ma', 'band'))
Inputs may be any that keep to these rules, and one draw needn't show every extreme that they name: `cycle_cell`: Band-local cycle; every point held by device (ma, band) lies in latitude band `band`. For each device and each ma index q, at most 16 of its points have cycles q * 4 to q * 4 + 3, and in every band one q receives exactly 16 points from every device of the band.
All inputs are finite; a program needn't handle non-finite values.
Results may differ from a plain program's by a relative error of at most 0.0053.
Values may be sent and summed in bfloat16 or wider, within the bound.
No kernel may reach another device: no remote copies, remote signals or barrier semaphores. Data moves between devices by JAX's collectives and lax.ppermute only.
A program may use at most 64 MiB of HBM per device.

v0:
```python
import jax
import jax.numpy as jnp
from jax import lax
from jax.sharding import PartitionSpec as P

NPHI = 128
TAPS = 8


def kernel_taps(shifts):
    return jnp.sinc(shifts) * jnp.sinc(shifts / 4.0)


def combine_parts(plus_part, minus_part):
    q_real = -(plus_part[:, 0, 0] - minus_part[:, 1, 1])
    q_imag = -(plus_part[:, 0, 1] + minus_part[:, 1, 0])
    u_real = -(plus_part[:, 1, 0] + minus_part[:, 0, 1])
    u_imag = -(plus_part[:, 1, 1] - minus_part[:, 0, 0])
    real_part = jnp.concatenate([q_real, u_real], axis=1)
    imag_part = jnp.concatenate([q_imag, u_imag], axis=1)
    return jnp.stack([real_part, imag_part], axis=1).astype(jnp.bfloat16)


def phase_table(m_values, cell_count, lmax_width):
    pixel_index = jnp.arange(cell_count, dtype=jnp.int32)
    period = 2 * lmax_width
    phase_turns = m_values[None, :] * pixel_index[:, None] % period
    angles = phase_turns.astype(jnp.float32) * (2.0 * jnp.pi / period)
    return jnp.stack([jnp.cos(angles), -jnp.sin(angles)], axis=-1).astype(jnp.bfloat16)


def spread_weights(starts, weights, length):
    tap_index = jnp.arange(TAPS, dtype=jnp.int32)
    target = starts[:, None] + tap_index[None, :]
    cells = jnp.arange(length, dtype=jnp.int32)
    hits = (target[:, :, None] == cells[None, None, :]).astype(jnp.float32)
    return jnp.sum(weights[:, :, None] * hits, axis=1)


def on_device(harmonics, legendre, m_values, cycle_cell, phi_cell, offsets):
    evolutions = harmonics.shape[2] // 4
    cycle_total = legendre.shape[3]
    owner_count = lax.axis_size("ma")
    band_count = lax.axis_size("band")
    cycle_depth = cycle_total // (owner_count * band_count)
    band_rows = owner_count * cycle_depth
    both = lax.dot_general(
        legendre[0], harmonics[0], (((1,), (0,)), ((), ())), preferred_element_type=jnp.float32
    )
    spectra = combine_parts(
        both[0].reshape(cycle_total, 2, 2, evolutions),
        both[1].reshape(cycle_total, 2, 2, evolutions),
    )
    width_out = spectra.shape[2]
    blocks = owner_count * band_count
    send = spectra.reshape(blocks, cycle_depth, 2, width_out).transpose(0, 2, 1, 3)
    received = lax.all_to_all(send, ("ma", "band"), split_axis=0, concat_axis=0, tiled=True)
    phase_rows = phase_table(m_values, NPHI, harmonics.shape[1])
    own = jnp.dot(
        phase_rows.reshape(NPHI, blocks * 2),
        received.reshape(blocks * 2, cycle_depth * width_out),
        preferred_element_type=jnp.float32,
    )
    own = (2.0 * own).astype(jnp.bfloat16).reshape(NPHI, cycle_depth, width_out)
    own = own.transpose(1, 0, 2)
    field = lax.all_gather(own, "ma", axis=0, tiled=True)
    tap_shift = jnp.arange(TAPS).astype(jnp.float32) - 3.0
    across = kernel_taps(tap_shift[None, :] - offsets[0][:, None])
    beside_all = kernel_taps(tap_shift[None, :] - offsets[1][:, None])
    cycle_weights = spread_weights(cycle_cell - 3, across, band_rows)
    phi_weights = spread_weights(phi_cell - 3, beside_all, NPHI)
    dense = (cycle_weights[:, :, None] * phi_weights[:, None, :]).astype(jnp.bfloat16)
    points = dense.shape[0]
    return jnp.dot(
        dense.reshape(points, band_rows * NPHI),
        field.reshape(band_rows * NPHI, width_out),
        preferred_element_type=jnp.float32,
    )


def solution(mesh):
    in_specs = (
        P(("ma", "band"), None, None),
        P(("ma", "band"), None, None, None),
        P(),
        P(("ma", "band")),
        P(("ma", "band")),
        P(None, ("ma", "band")),
    )
    out_specs = P(("ma", "band"), None)
    return jax.shard_map(
        on_device, mesh=mesh, in_specs=in_specs, out_specs=out_specs, check_vma=False
    )
```

profile of v0, /device:TPU:0, one launch (start us, length us, event | category | flops | bytes accessed | tf_op | source)
XLA Modules:
  0.0 93.0 jit_solution(1957809153927481940)
XLA Ops:
  6.5 9.4 %fusion = f32[2,512,256]{1,2,0:T(8,128)S(1)} fusion(bf16[1,2,8192,512]{3,2,1,0:T(8,128)(2,1)} %param.8, bf16[1,8192,256]{2,1,0:T(8,128)(2,1)} %param.7), kind=kOutput, calls=%fused_computation | convolution fusion | flops 4294967296 | bytes 22020096 | tf_op jit(solution)/shard_map/dot_general | solution.py:47
  15.9 0.1 fusion.103
  16.0 0.1 copy.58
  16.2 0.0 copy-start.1
  16.2 0.0 copy-start
  16.2 0.0 copy-start.2
  16.3 0.0 copy-start.3
  16.3 0.1 copy.59
  16.4 0.1 copy.60
  16.5 0.1 copy.61
  16.7 0.1 copy.62
  16.8 0.1 copy.63
  16.9 0.1 copy.64
  17.1 0.1 copy.65
  17.4 0.4 maximum_bitcast_fusion
  17.7 0.8 copy.54
  18.5 11.2 %all-to-all-start = ((bf16[128,2,4,128]{3,2,1,0:T(4,128)(2,1)}), bf16[128,2,4,128]{3,2,1,0:T(4,128)(2,1)S(1)}, u32[]{:S(2)}, u32[]{:S(2)}) async-start(bf16[128,2,4,128]{3,2,1,0:T(4,128)(2,1)} %copy.54), calls=%async_computation | async-start | bytes 524288 | tf_op jit(solution)/shard_map/all_to_all | solution.py:57
  29.7 0.0 all-gather.2.cloned.1.call-start
  29.8 0.0 copy-done.1
  29.8 0.3 cosine_convert_fusion
  30.1 0.1 copy.44
  30.2 10.2 %all-to-all-done = bf16[128,2,4,128]{3,2,1,0:T(4,128)(2,1)S(1)} async-done(((bf16[128,2,4,128]{3,2,1,0:T(4,128)(2,1)}), bf16[128,2,4,128]{3,2,1,0:T(4,128)(2,1)S(1)}, u32[]{:S(2)}, u32[]{:S(2)}) %all-to-all-start) | async-done | bytes 262176 | tf_op jit(solution)/shard_map/all_to_all | solution.py:57
  40.4 0.2 fusion.7
  40.7 0.7 copy.73
  41.3 0.0 all-gather.2.cloned.1.call-update
  41.4 0.0 copy-done
  41.4 0.1 fusion.41
  41.5 0.1 copy.43
  41.7 0.1 iota_add_fusion
  41.8 0.3 select_reduce_fusion
  42.1 40.5 %all-gather.2.cloned.1.call-done = bf16[64,128,128]{2,1,0:T(8,128)(2,1)} async-done(((bf16[4,128,128]{2,1,0:T(8,128)(2,1)}), bf16[64,128,128]{2,1,0:T(8,128)(2,1)}) %all-gather.2.cloned.1.call-update) | async-done | bytes 2097168 | tf_op jit(solution)/shard_map/all_gather | solution.py:66
  82.6 3.5 %fusion.8 = f32[128,128]{1,0:T(8,128)} fusion(bf16[64,128,128]{2,1,0:T(8,128)(2,1)} %all-gather.2.cloned.1.call-done, f32[128,128]{1,0:T(8,128)S(1)} %select_reduce_fusion, f32[128,64]{0,1:T(8,128)S(1)} %select_reduce_fusion.1), kind=kOutput, calls=%fused_computation.10 | convolution fusion | flops 270532608 | bytes 2260992 | tf_op jit(solution)/shard_map/dot_general | solution.py:74
  (15 shorter events, 0.3 us)
Async XLA Ops:
  16.2 13.6 %copy-start.1 = (s32[128]{0:T(128)S(1)}, s32[128]{0:T(128)}, u32[]{:S(2)}) copy-start(s32[128]{0:T(128)} %param.9) | copy-start | bytes 1540
  16.2 25.1 %copy-start = (f32[2,128]{1,0:T(2,128)S(1)}, f32[2,128]{1,0:T(2,128)}, u32[]{:S(2)}) copy-start(f32[2,128]{1,0:T(2,128)} %param.12) | copy-start | bytes 3076
  16.2 25.3 %copy-start.2 = (s32[128]{0:T(128)S(1)}, s32[128]{0:T(128)}, u32[]{:S(2)}) copy-start(s32[128]{0:T(128)} %param.10) | copy-start | bytes 1540
  16.3 25.4 %copy-start.3 = (s32[128]{0:T(128)S(1)}, s32[128]{0:T(128)}, u32[]{:S(2)}) copy-start(s32[128]{0:T(128)} %param.11) | copy-start | bytes 1540
  18.5 21.9 %all-to-all-start = ((bf16[128,2,4,128]{3,2,1,0:T(4,128)(2,1)}), bf16[128,2,4,128]{3,2,1,0:T(4,128)(2,1)S(1)}, u32[]{:S(2)}, u32[]{:S(2)}) async-start(bf16[128,2,4,128]{3,2,1,0:T(4,128)(2,1)} %copy.54), calls=%async_computation | async-start | bytes 524288 | tf_op jit(solution)/shard_map/all_to_all | solution.py:57
  29.7 52.9 %all-gather.2.cloned.1.call-start = ((), (), s32[]{:S(2)}) async-start(), calls=%async_computation.1 | async-start | bytes 2228224 | tf_op jit(solution)/shard_map/all_gather | solution.py:66
Sparse Core Ops, SparseCore 0:
  41.5 41.1 all-gather.1
where the time goes:
time: 93.2 us; the launch traced here: 93 us
  waiting for transfers between devices  50.8 us (55%)
  between operations  13.7 us (15%)
  matrix products  13.1 us (14%)
  starting transfers between devices  11.2 us (12%)
  local copies, waits for them, and re-layouts  2.87 us (3%)
  other arithmetic  1.37 us (1%)
    all_gather x1, waiting for transfers between devices, on_device(): field = lax.all_gather(own, 'ma', axis=0, tiled=True)  40.5 us
    all_to_all x1, starting transfers between devices, on_device(): lax.all_to_all(send, ('ma', 'band'), split_axis=0, concat_axis=0, tiled=T...  11.2 us
    all_to_all x1, waiting for transfers between devices, on_device(): lax.all_to_all(send, ('ma', 'band'), split_axis=0, concat_axis=0, tiled=T...  10.2 us
    dot_general x1, matrix products, on_device(): lax.dot_general(legendre[0], harmonics[0], (((1,), (0,)), ((), ())), pref...  9.38 us
    dot_general x1, matrix products, on_device(): jnp.dot(dense.reshape(points, band_rows * NPHI), field.reshape(band_rows...  3.5 us
  transfers between devices with their start and end apart: 2, of which 2 were waited for; matrix products, arithmetic and copies ran while one was open for 1% of the time, Pallas kernels for 0%

commit v1 on v0

--- a/solution.py
+++ b/solution.py
@@ -2,6 +2,7 @@
 import jax.numpy as jnp
 from jax import lax
 from jax.sharding import PartitionSpec as P
+from jax.lax import all_to_all, axis_size
 
 NPHI = 128
 TAPS = 8
@@ -63,7 +64,8 @@
     )
     own = (2.0 * own).astype(jnp.bfloat16).reshape(NPHI, cycle_depth, width_out)
     own = own.transpose(1, 0, 2)
-    field = lax.all_gather(own, "ma", axis=0, tiled=True)
+    back = jnp.stack([own] * axis_size("ma"), axis=0)
+    field = jnp.concatenate(all_to_all(back, axis_name="ma", split_axis=0, concat_axis=0), 0)
     tap_shift = jnp.arange(TAPS).astype(jnp.float32) - 3.0
     across = kernel_taps(tap_shift[None, :] - offsets[0][:, None])
     beside_all = kernel_taps(tap_shift[None, :] - offsets[1][:, None])

time: 93.2 us -> 74 us (0.79)
  between operations: 13.7 us -> 0.29 us
  waiting for transfers between devices: 50.8 us -> 37.4 us
  starting transfers between devices: 11.2 us -> 14.9 us
  other arithmetic: 1.37 us -> 3.7 us
  local copies, waits for them, and re-layouts: 2.87 us -> 4.18 us
    all_gather x1 -> x0, waiting for transfers between devices: 40.5 us -> none  [on_device(): field = lax.all_gather(own, 'ma', axis=0, tiled=True)]
    all_to_all x0 -> x1, waiting for transfers between devices: none -> 27.1 us  [on_device(): all_to_all(back, axis_name='ma', split_axis=0, concat_axis=0)]
    all_to_all x0 -> x1, starting transfers between devices: none -> 3.72 us  [on_device(): all_to_all(back, axis_name='ma', split_axis=0, concat_axis=0)]
    convert_element_type x0 -> x1, other arithmetic: none -> 2.34 us  [on_device(): (cycle_weights[:, :, None] * phi_weights[:, None, :]).astype(jnp.bfloat16)]
    another operation x0 -> x1, local copies, waits for them, and re-layouts: none -> 1.85 us  [on_device(): back = jnp.stack([own] * axis_size('ma'), axis=0)]
  transfers between devices with their start and end apart: 2 -> 2, of which waited for: 2 -> 2; matrix products, arithmetic and copies ran while one was open for 1% -> 5% of each run, Pallas kernels for 0% -> 0%
where the time goes in v1:
time: 74 us; the launch traced here: 73.7 us
  waiting for transfers between devices  37.4 us (51%)
  starting transfers between devices  14.9 us (20%)
  matrix products  13.3 us (18%)
  local copies, waits for them, and re-layouts  4.18 us (6%)
  other arithmetic  3.7 us (5%)
    all_to_all x1, waiting for transfers between devices, on_device(): all_to_all(back, axis_name='ma', split_axis=0, concat_axis=0)  27.1 us
    all_to_all x1, starting transfers between devices, on_device(): lax.all_to_all(send, ('ma', 'band'), split_axis=0, concat_axis=0, tiled=T...  11.2 us
    all_to_all x1, waiting for transfers between devices, on_device(): lax.all_to_all(send, ('ma', 'band'), split_axis=0, concat_axis=0, tiled=T...  10.3 us
    dot_general x1, matrix products, on_device(): lax.dot_general(legendre[0], harmonics[0], (((1,), (0,)), ((), ())), pref...  9.39 us
    all_to_all x1, starting transfers between devices, on_device(): all_to_all(back, axis_name='ma', split_axis=0, concat_axis=0)  3.72 us
    dot_general x1, matrix products, on_device(): jnp.dot(dense.reshape(points, band_rows * NPHI), field.reshape(band_rows...  3.66 us
    convert_element_type x1, other arithmetic, on_device(): (cycle_weights[:, :, None] * phi_weights[:, None, :]).astype(jnp.bfloat16)  2.34 us
    another operation x1, local copies, waits for them, and re-layouts, on_device(): back = jnp.stack([own] * axis_size('ma'), axis=0)  1.85 us
  transfers between devices with their start and end apart: 2, of which 2 were waited for; matrix products, arithmetic and copies ran while one was open for 5% of the time, Pallas kernels for 0%

profile of v1, /device:TPU:0, one launch (start us, length us, event | category | flops | bytes accessed | tf_op | source)
XLA Modules:
  0.0 73.7 jit_solution(4081525475157221817)
XLA Ops:
  0.0 9.4 %fusion = f32[2,512,256]{1,2,0:T(8,128)S(1)} fusion(bf16[1,2,8192,512]{3,2,1,0:T(8,128)(2,1)} %param.8, bf16[1,8192,256]{2,1,0:T(8,128)(2,1)} %param.7), kind=kOutput, calls=%fused_computation | convolution fusion | flops 4294967296 | bytes 22020096 | tf_op jit(solution)/shard_map/dot_general | solution.py:48
  9.4 0.1 fusion.101
  9.5 0.1 copy.60
  9.6 0.0 copy-start.1
  9.7 0.1 copy.61
  9.8 0.1 copy.62
  10.0 0.1 copy.63
  10.1 0.1 copy.64
  10.2 0.1 copy.65
  10.4 0.1 copy.66
  10.5 0.1 copy.67
  10.8 0.4 maximum_bitcast_fusion
  11.2 0.8 %copy.56 = bf16[128,2,4,128]{3,2,1,0:T(4,128)(2,1)} copy(bf16[128,2,4,128]{3,2,0,1:T(4,128)(2,1)S(1)} %maximum_bitcast_fusion) | data formatting | bytes 524288 | tf_op jit(solution)/shard_map/transpose | solution.py:57
  12.0 11.2 %all-to-all-start = ((bf16[128,2,4,128]{3,2,1,0:T(4,128)(2,1)}), bf16[128,2,4,128]{3,2,1,0:T(4,128)(2,1)S(1)}, u32[]{:S(2)}, u32[]{:S(2)}) async-start(bf16[128,2,4,128]{3,2,1,0:T(4,128)(2,1)} %copy.56), calls=%async_computation | async-start | bytes 524288 | tf_op jit(solution)/shard_map/all_to_all | solution.py:58
  23.1 0.0 copy-done.1
  23.2 0.3 cosine_convert_fusion
  23.5 0.1 copy.46
  23.6 10.3 %all-to-all-done = bf16[128,2,4,128]{3,2,1,0:T(4,128)(2,1)S(1)} async-done(((bf16[128,2,4,128]{3,2,1,0:T(4,128)(2,1)}), bf16[128,2,4,128]{3,2,1,0:T(4,128)(2,1)S(1)}, u32[]{:S(2)}, u32[]{:S(2)}) %all-to-all-start) | async-done | bytes 262176 | tf_op jit(solution)/shard_map/all_to_all | solution.py:58
  33.9 0.2 fusion.6
  34.2 1.9 %stack.9 = bf16[16,4,128,128]{3,2,1,0:T(8,128)(2,1)} broadcast(bf16[4,128,128]{2,1,0:T(8,128)(2,1)S(1)} %copy.57), dimensions={1,2,3} | broadcast | bytes 2228224 | tf_op jit(solution)/shard_map/stack | solution.py:67
  36.0 3.7 %all-to-all-start.1 = ((bf16[16,4,128,128]{3,2,1,0:T(8,128)(2,1)}), bf16[16,4,128,128]{3,2,1,0:T(8,128)(2,1)S(1)}, u32[]{:S(2)}, u32[]{:S(2)}) async-start(bf16[16,4,128,128]{3,2,1,0:T(8,128)(2,1)} %stack.9), calls=%async_computation.1 | async-start | bytes 4194304 | tf_op jit(solution)/shard_map/all_to_all | solution.py:68
  39.7 0.0 copy-done
  39.8 0.1 fusion.39
  39.9 0.1 copy.45
  40.0 0.0 copy-done.2
  40.0 0.1 copy.44
  40.1 0.0 copy-done.3
  40.2 0.1 iota_add_fusion
  40.2 0.3 select_reduce_fusion
  40.6 2.3 %multiply_convert_fusion = bf16[128,64,128]{2,1,0:T(8,128)(2,1)} fusion(f32[128,128]{1,0:T(8,128)S(1)} %select_reduce_fusion, f32[128,64]{1,0:T(8,128)S(1)} %copy.44), kind=kLoop, calls=%fused_computation.3 | loop fusion | flops 2097152 | bytes 2195456 | tf_op jit(solution)/shard_map/convert_element_type | solution.py:74
  42.9 27.1 %all-to-all-done.1 = bf16[16,4,128,128]{3,2,1,0:T(8,128)(2,1)S(1)} async-done(((bf16[16,4,128,128]{3,2,1,0:T(8,128)(2,1)}), bf16[16,4,128,128]{3,2,1,0:T(8,128)(2,1)S(1)}, u32[]{:S(2)}, u32[]{:S(2)}) %all-to-all-start.1) | async-done | bytes 2097184 | tf_op jit(solution)/shard_map/all_to_all | solution.py:68
  70.1 3.7 %fusion.3 = f32[128,128]{1,0:T(8,128)} fusion(bf16[8192,128]{1,0:T(8,128)(2,1)S(1)} %bitcast.34, bf16[16,8,64,128]{3,2,1,0:T(8,128)(2,1)} %bitcast.35), kind=kOutput, calls=%fused_computation.4 | convolution fusion | flops 268435456 | bytes 4259840 | tf_op jit(solution)/shard_map/dot_general | solution.py:76
  (18 shorter events, 0.3 us)
Async XLA Ops:
  9.6 13.5 %copy-start.1 = (s32[128]{0:T(128)S(1)}, s32[128]{0:T(128)}, u32[]{:S(2)}) copy-start(s32[128]{0:T(128)} %param.9) | copy-start | bytes 1540
  12.0 27.8 %copy-start = (f32[2,128]{1,0:T(2,128)S(1)}, f32[2,128]{1,0:T(2,128)}, u32[]{:S(2)}) copy-start(f32[2,128]{1,0:T(2,128)} %param.12) | copy-start | bytes 3076
  12.0 28.0 %copy-start.2 = (s32[128]{0:T(128)S(1)}, s32[128]{0:T(128)}, u32[]{:S(2)}) copy-start(s32[128]{0:T(128)} %param.10) | copy-start | bytes 1540
  12.0 28.2 %copy-start.3 = (s32[128]{0:T(128)S(1)}, s32[128]{0:T(128)}, u32[]{:S(2)}) copy-start(s32[128]{0:T(128)} %param.11) | copy-start | bytes 1540
  12.0 21.9 %all-to-all-start = ((bf16[128,2,4,128]{3,2,1,0:T(4,128)(2,1)}), bf16[128,2,4,128]{3,2,1,0:T(4,128)(2,1)S(1)}, u32[]{:S(2)}, u32[]{:S(2)}) async-start(bf16[128,2,4,128]{3,2,1,0:T(4,128)(2,1)} %copy.56), calls=%async_computation | async-start | bytes 524288 | tf_op jit(solution)/shard_map/all_to_all | solution.py:58
  36.0 34.1 %all-to-all-start.1 = ((bf16[16,4,128,128]{3,2,1,0:T(8,128)(2,1)}), bf16[16,4,128,128]{3,2,1,0:T(8,128)(2,1)S(1)}, u32[]{:S(2)}, u32[]{:S(2)}) async-start(bf16[16,4,128,128]{3,2,1,0:T(8,128)(2,1)} %stack.9), calls=%async_computation.1 | async-start | bytes 4194304 | tf_op jit(solution)/shard_map/all_to_all | solution.py:68
